TPU v7x, 32 devices: a whole 2x2x4 slice. The times are simulated.
32 devices in a mesh: groups: 2 (over y), space: 8 (over z, x), tm: 2 (over core).
Axes of the slice: x: 2, y: 2, z: 4, core: 2. Of those that a mesh axis runs over, the one named last changes fastest.
Arguments:
- latents: bfloat16 [4, 16, 4, 256, 256], P('groups', 'space', 'tm'), parts along dimension 0, may hold values from -6 to 6
- cotangent: bfloat16 [4, 16, 4, 256, 256], P('groups', 'space', 'tm'), parts along dimension 0, may hold values from -6 to 6
- valid_frames: int32 [4], P('groups'), parts along dimension 0, may hold values from 1 to 16, as said below
- spatial_weight: bfloat16 [9, 256, 256], replicated, may hold values from -0.125 to 0.125
- temporal_weight: bfloat16 [3, 256, 256], replicated, may hold values from -0.21875 to 0.21875
- cond_weight: bfloat16 [256, 256], replicated, may hold values from -0.375 to 0.375
Outputs:
- output: bfloat16 [4, 16, 4, 256, 256], P('groups', 'space', 'tm'), parts along dimension 0
- grad_latents: bfloat16 [4, 16, 4, 256, 256], P('groups', 'space', 'tm'), parts along dimension 0
- grad_spatial: bfloat16 [18, 256, 256], P('groups'), parts along dimension 0
- grad_temporal: bfloat16 [6, 256, 256], P('groups'), parts along dimension 0
- grad_cond: bfloat16 [512, 256], P('groups'), parts along dimension 0
There are 2 independent parts, one for each index of `groups`. A program takes and returns all parts, laid end to end along the dimension named above; an argument that names none is the same for every part. Nothing has to cross between parts.
Inputs may be any that keep to these rules, and one draw needn't show every extreme that they name: `valid_frames`: the first clip has all 16 frames valid; the others have 1 to 16.
All inputs are finite; a program needn't handle non-finite values.
Results may differ from a plain program's by a relative error of at most 0.0055.
Values may be sent and summed in bfloat16 or wider, within the bound.
No kernel may reach another device: no remote copies, remote signals or barrier semaphores. Data moves between devices by JAX's collectives and lax.ppermute only.
A program may use at most 128 MiB of HBM per device.

v0:
```python
import jax
import jax.numpy as jnp
from jax import lax
from jax.sharding import PartitionSpec as P


def from_root(block, axis, source):
    block = jnp.where(lax.axis_index(axis) == source, block, jnp.zeros_like(block))
    return lax.psum(block, axis)


def shifted(value, axis, by):
    count = lax.axis_size(axis)
    pairs = [(i, i + by) for i in range(count) if 0 <= i + by < count]
    return lax.ppermute(value, axis, pairs)


def spatial_sum(padded, weights, flip):
    rows = padded.shape[2] - 2
    cols = padded.shape[3] - 2
    total = jnp.zeros(padded.shape[:2] + (rows, cols, weights.shape[2]), jnp.float32)
    for row_off in range(3):
        for col_off in range(3):
            if flip:
                piece = padded[
                    :, :, 2 - row_off : 2 - row_off + rows, 2 - col_off : 2 - col_off + cols
                ]
                kernel = weights[3 * row_off + col_off].T
            else:
                piece = padded[:, :, row_off : row_off + rows, col_off : col_off + cols]
                kernel = weights[3 * row_off + col_off]
            total = total + jnp.dot(piece, kernel, preferred_element_type=jnp.float32)
    return total


def lag_forward(padded_act, weights, count):
    total = 0.0
    for lag in range(3):
        total = total + jnp.dot(
            padded_act[:, 2 - lag : 2 - lag + count],
            weights[lag],
            preferred_element_type=jnp.float32,
        )
    return total


def lag_backward(padded_cot, weights, count):
    total = 0.0
    for lag in range(3):
        total = total + jnp.dot(
            padded_cot[:, lag : lag + count], weights[lag].T, preferred_element_type=jnp.float32
        )
    return total


def lag_grads(padded_act, cot, count):
    dims = (((0, 1, 2, 3), (0, 1, 2, 3)), ((), ()))
    terms = []
    for lag in range(3):
        terms.append(
            lax.dot_general(
                padded_act[:, 2 - lag : 2 - lag + count],
                cot,
                dims,
                preferred_element_type=jnp.float32,
            )
        )
    return jnp.stack(terms)


def own_window(whole, rows):
    padded_rows = jnp.pad(whole, ((0, 0), (0, 0), (1, 1), (0, 0), (0, 0)))
    start = lax.axis_index("tm") * rows
    return lax.dynamic_slice_in_dim(padded_rows, start, rows + 2, 2)


def on_device(latents, cotangent, valid_frames, spatial_weight, temporal_weight, cond_weight):
    clips, frames, rows, cols, chans = latents.shape
    slab = lax.axis_index("space")
    frame_ids = slab * frames + jnp.arange(frames, dtype=jnp.int32)
    mask = (frame_ids[None, :] < valid_frames[:, None]).astype(jnp.bfloat16)[:, :, None, None, None]
    mask_f = mask.astype(jnp.float32)
    masked = latents * mask
    first = from_root(masked[:, 0], "space", 0)
    rows_pad = own_window(lax.all_gather(masked, "tm", axis=2, tiled=True), rows)
    padded = jnp.pad(rows_pad, ((0, 0), (0, 0), (0, 0), (1, 1), (0, 0)))
    pre = spatial_sum(padded, spatial_weight, False)
    act = jax.nn.silu(pre).astype(jnp.bfloat16)
    cot = cotangent * mask
    earlier = shifted(act, "space", 1)
    act_pad = jnp.concatenate([earlier, act], axis=1)
    mixed = lag_forward(act_pad, temporal_weight, frames)
    later = shifted(cot, "space", -1)
    cot_pad = jnp.concatenate([cot, later], axis=1)
    dact = lag_backward(cot_pad, temporal_weight, frames)
    temporal_terms = lag_grads(act_pad, cot, frames)
    cond = jnp.dot(first, cond_weight, preferred_element_type=jnp.float32)
    output = ((masked.astype(jnp.float32) + mixed + cond[:, None]) * mask_f).astype(jnp.bfloat16)
    sig = jax.nn.sigmoid(pre)
    dpre = (dact * sig * (1.0 + pre * (1.0 - sig))).astype(jnp.bfloat16)
    cot_sum = lax.psum(jnp.sum(cot, axis=1, dtype=jnp.float32), "space")
    cond_back = jnp.dot(cot_sum, cond_weight.astype(jnp.float32).T, precision=lax.Precision.HIGHEST)
    dpre_rows = own_window(lax.all_gather(dpre, "tm", axis=2, tiled=True), rows)
    dpre_pad = jnp.pad(dpre_rows, ((0, 0), (0, 0), (0, 0), (1, 1), (0, 0)))
    dmasked = spatial_sum(dpre_pad, spatial_weight, True)
    is_first = (frame_ids == 0).astype(jnp.float32)[None, :, None, None, None]
    grad_latents = (
        (cot.astype(jnp.float32) + dmasked + is_first * cond_back[:, None]) * mask_f
    ).astype(jnp.bfloat16)
    dims = (((0, 1, 2, 3), (0, 1, 2, 3)), ((), ()))
    spatial_terms = []
    for row_off in range(3):
        for col_off in range(3):
            piece = padded[:, :, row_off : row_off + rows, col_off : col_off + cols]
            spatial_terms.append(
                lax.dot_general(piece, dpre, dims, preferred_element_type=jnp.float32)
            )
    spatial_terms = jnp.stack(spatial_terms)
    is_owner = (slab == 0).astype(jnp.float32)
    cond_terms = is_owner * lax.dot_general(
        first.astype(jnp.float32),
        cot_sum,
        (((0, 1, 2), (0, 1, 2)), ((), ())),
        precision=lax.Precision.HIGHEST,
    )
    summed = lax.psum((spatial_terms, temporal_terms, cond_terms), ("space", "tm"))
    scale = (clips * frames * rows * cols * lax.axis_size("space") * lax.axis_size("tm")) ** (-0.5)
    grad_spatial = (summed[0] * scale).astype(jnp.bfloat16)
    grad_temporal = (summed[1] * scale).astype(jnp.bfloat16)
    grad_cond = (summed[2] * scale).astype(jnp.bfloat16)
    return (output, grad_latents, grad_spatial, grad_temporal, grad_cond)


def solution(mesh):
    return jax.shard_map(
        on_device,
        mesh=mesh,
        in_specs=(
            P("groups", "space", "tm", None, None),
            P("groups", "space", "tm", None, None),
            P("groups"),
            P(),
            P(),
            P(),
        ),
        out_specs=(
            P("groups", "space", "tm", None, None),
            P("groups", "space", "tm", None, None),
            P("groups", None, None),
            P("groups", None, None),
            P("groups", None),
        ),
        check_vma=False,
    )
```

profile of v0, /device:TPU:0, one launch (start us, length us, event | category | flops | bytes accessed | tf_op | source)
XLA Modules:
  0.0 338.7 jit_solution(10557166967447815481)
XLA Ops:
  8.1 0.7 fusion.124
  8.8 1.4 broadcast_multiply_fusion.1
  10.2 0.9 fusion.44
  11.2 2.7 convert_reduce_fusion
  14.0 0.5 all-gather.3.cloned.1.call-update
  14.5 1.3 collective-permute-start.1
  15.9 1.8 fusion.75
  17.7 75.7 %all-reduce.9.cloned.1.call-done = bf16[2,2,256,256]{3,2,1,0:T(8,128)(2,1)} async-done(((bf16[2,2,256,256]{3,2,1,0:T(8,128)(2,1)}), bf16[2,2,256,256]{3,2,1,0:T(8,128)(2,1)}) %all-reduce.9.cloned.1.call-update) | async-done | bytes 524304 | tf_op jit(solution)/shard_map/psum | solution.py:9
  93.3 2.3 fusion.47
  95.7 79.6 %all-reduce.11.cloned.1.call-done = f32[2,2,256,256]{3,2,1,0:T(8,128)} async-done(((f32[2,2,256,256]{3,2,1,0:T(8,128)}), f32[2,2,256,256]{3,2,1,0:T(8,128)}) %all-reduce.11.cloned.1.call-update) | async-done | bytes 1048592 | tf_op jit(solution)/shard_map/psum | solution.py:101
  175.3 3.0 fusion.13
  178.2 1.6 fusion.45
  179.9 1.8 fusion.3
  181.7 1.8 pad_dynamic-slice_fusion.1
  183.5 0.4 fusion.38
  183.9 0.5 fusion.39
  184.4 0.5 fusion.40
  184.8 0.5 fusion.41
  185.3 0.5 fusion.42
  185.8 0.5 fusion.43
  186.2 0.4 fusion.59
  186.6 0.4 fusion.67
  187.1 2.1 multiply_convert_fusion.3
  189.4 0.5 copy-done.24
  189.9 2.0 multiply_convert_fusion.1
  191.9 1.2 fusion.19
  193.2 3.5 %collective-permute-start = (bf16[2,2,2,256,256]{4,3,2,1,0:T(8,128)(2,1)}, bf16[2,2,2,256,256]{4,3,2,1,0:T(8,128)(2,1)S(1)}, u32[]{:S(2)}, u32[]{:S(2)}) collective-permute-start(bf16[2,2,2,256,256]{4,3,2,1,0:T(8,128)(2,1)} %get-tuple-element.12), channel_id=1, source_target_pairs={{0,2},{2,4},{4,6},{6,8},{8,10},{10,12},{12,14},{1,3},{3,5},{5,7},{... | collective-permute-start | bytes 3145736 | tf_op jit(solution)/shard_map/ppermute | solution.py:15
  196.7 2.4 fusion.12
  199.1 1.2 fusion.18
  200.3 1.2 fusion.17
  201.5 1.2 fusion.11
  202.7 1.2 fusion.16
  203.8 1.2 fusion.15
  205.1 0.4 copy-done.7
  205.5 0.5 convolution_bitcast_fusion.5
  205.9 1.2 fusion.10
  207.1 1.2 fusion.14
  208.3 2.7 fusion.77
  211.0 7.8 %collective-permute-done = bf16[2,2,2,256,256]{4,3,2,1,0:T(8,128)(2,1)S(1)} collective-permute-done((bf16[2,2,2,256,256]{4,3,2,1,0:T(8,128)(2,1)}, bf16[2,2,2,256,256]{4,3,2,1,0:T(8,128)(2,1)S(1)}, u32[]{:S(2)}, u32[]{:S(2)}) %collective-permute-start) | collective-permute-done | bytes 1048608 | tf_op jit(solution)/shard_map/ppermute | solution.py:15
  218.9 0.5 convolution_bitcast_fusion.4
  219.3 0.5 fusion.9
  219.8 1.0 pad_maximum_fusion.5
  220.8 1.2 copy-done.8
  222.0 0.3 copy-done.10
  222.4 0.4 fusion.7
  222.9 0.8 copy-done.12
  223.7 0.7 copy-done.13
  224.6 1.7 multiply_convert_fusion.2
  226.3 1.8 pad_dynamic-slice_fusion
  228.2 0.5 fusion.20
  228.6 0.5 fusion.22
  229.1 0.5 fusion.24
  229.6 0.5 fusion.26
  230.1 0.5 fusion.28
  230.6 0.5 fusion.30
  231.1 0.5 fusion.57
  231.6 0.5 fusion.65
  232.0 0.8 copy-done.6
  232.8 0.3 copy-done.16
  233.1 2.2 fusion.2
  235.3 91.7 %all-reduce.13.cloned.1.call-done = (f32[9,256,256]{2,1,0:T(8,128)}, f32[3,256,256]{2,1,0:T(8,128)}, f32[256,256]{1,0:T(8,128)}) async-done(((f32[9,256,256]{2,1,0:T(8,128)}, f32[3,256,256]{2,1,0:T(8,128)}, f32[256,256]{1,0:T(8,128)}), (f32[9,256,256]{2,1,0:T(8,128)}, f32[3,256,256]{2,1,0:T(8,128)}, f32[256,256]{1,0:T(8,128)})) %all-reduce.13.cloned.1.call-update) | async-done | bytes 3407888 | tf_op jit(solution)/shard_map/psum | solution.py:126
  327.0 3.0 multiply_convert_fusion
  330.0 0.8 multiply_convert_fusion.4
  330.9 0.7 multiply_convert_fusion.5
  (60 shorter events, 0.9 us)
Async XLA Ops:
  8.0 85.3 %copy-start = (bf16[256,256]{1,0:T(8,128)(2,1)S(1)}, bf16[256,256]{1,0:T(8,128)(2,1)}, u32[]{:S(2)}) copy-start(bf16[256,256]{1,0:T(8,128)(2,1)} %param.11) | copy-start | bytes 393220
  8.0 85.3 %all-reduce.9.cloned.1.call-start = ((), (), s32[]{:S(2)}) async-start(), calls=%async_computation.1 | async-start | bytes 1048576 | tf_op jit(solution)/shard_map/psum | solution.py:9
  10.2 3.7 %copy-start.11 = (bf16[2,2,2,256,256]{4,3,2,1,0:T(8,128)(2,1)}, bf16[2,2,2,256,256]{4,3,2,1,0:T(8,128)(2,1)S(1)}, u32[]{:S(2)}) copy-start(bf16[2,2,2,256,256]{4,3,2,1,0:T(8,128)(2,1)S(1)} %broadcast_multiply_fusion.1) | copy-start | bytes 3145732
  11.1 4.8 %copy-start.21 = (bf16[3,256,256]{2,1,0:T(8,128)(2,1)S(1)}, bf16[3,256,256]{2,1,0:T(8,128)(2,1)}, u32[]{:S(2)}) copy-start(bf16[3,256,256]{2,1,0:T(8,128)(2,1)} %param.10) | copy-start | bytes 1179652
  11.1 164.2 %all-reduce.11.cloned.1.call-start = ((), (), s32[]{:S(2)}) async-start(), calls=%async_computation.3 | async-start | bytes 2097152 | tf_op jit(solution)/shard_map/psum | solution.py:101
  13.9 166.0 %copy-start.4 = (bf16[2,2,2,256,256]{4,3,2,1,0:T(8,128)(2,1)}, bf16[2,2,2,256,256]{4,3,2,1,0:T(8,128)(2,1)S(1)}, u32[]{:S(2)}) copy-start(bf16[2,2,2,256,256]{4,3,2,1,0:T(8,128)(2,1)S(1)} %get-tuple-element.9) | copy-start | bytes 3145732
  13.9 167.8 %all-gather.3.cloned.1.call-start = ((), (), s32[]{:S(2)}) async-start(), calls=%async_computation | async-start | bytes 3145728 | tf_op jit(solution)/shard_map/all_gather | solution.py:85
  14.5 211.8 %all-gather.5.cloned.1.call-start = ((), (), s32[]{:S(2)}) async-start(), calls=%async_computation.2 | async-start | bytes 3145728 | tf_op jit(solution)/shard_map/all_gather | solution.py:103
  14.5 165.3 %collective-permute-start.1 = (bf16[2,2,2,256,256]{4,3,2,1,0:T(8,128)(2,1)S(1)}, bf16[2,2,2,256,256]{4,3,2,1,0:T(8,128)(2,1)S(1)}, u32[]{:S(2)}, u32[]{:S(2)}) collective-permute-start(bf16[2,2,2,256,256]{4,3,2,1,0:T(8,128)(2,1)S(1)} %get-tuple-element.9), channel_id=1, source_target_pairs={{2,0},{4,2},{6,4},{8,6},{10,8},{12,10},{14,12},{3,1},{5,3},{7,5},{... | collective-permute-start | bytes 3145736 | tf_op jit(solution)/shard_map/ppermute | solution.py:15
  175.3 3.0 copy-start.18
  179.8 1.8 copy-start.23
  181.7 1.8 copy-start.14
  187.1 2.2 copy-start.19
  187.1 2.3 copy-start.20
  187.1 2.8 copy-start.24
  191.9 1.2 copy-start.2
  193.1 6.0 %copy-start.3 = (bf16[2,2,2,256,256]{4,3,2,1,0:T(8,128)(2,1)S(1)}, bf16[2,2,2,256,256]{4,3,2,1,0:T(8,128)(2,1)}, u32[]{:S(2)}) copy-start(bf16[2,2,2,256,256]{4,3,2,1,0:T(8,128)(2,1)} %copy-done.2) | copy-start | bytes 3145732
  193.2 133.8 %all-reduce.13.cloned.1.call-start = ((), (), s32[]{:S(2)}) async-start(), calls=%async_computation.4 | async-start | bytes 6815744 | tf_op jit(solution)/shard_map/psum | solution.py:126
  193.2 25.7 %collective-permute-start = (bf16[2,2,2,256,256]{4,3,2,1,0:T(8,128)(2,1)}, bf16[2,2,2,256,256]{4,3,2,1,0:T(8,128)(2,1)S(1)}, u32[]{:S(2)}, u32[]{:S(2)}) collective-permute-start(bf16[2,2,2,256,256]{4,3,2,1,0:T(8,128)(2,1)} %get-tuple-element.12), channel_id=1, source_target_pairs={{0,2},{2,4},{4,6},{6,8},{8,10},{10,12},{12,14},{1,3},{3,5},{5,7},{... | collective-permute-start | bytes 3145736 | tf_op jit(solution)/shard_map/ppermute | solution.py:15
  203.8 1.2 copy-start.5
  203.8 1.6 copy-start.7
  218.9 1.0 copy-start.9
  220.8 1.2 copy-start.8
  220.8 1.5 copy-start.10
  220.8 1.6 copy-start.22
  222.4 1.2 copy-start.12
  222.4 1.9 copy-start.13
  222.4 2.2 copy-start.17
  226.3 1.9 copy-start.15
  231.6 1.2 copy-start.6
  231.6 1.6 copy-start.16
  327.0 3.0 copy-start.25
  327.0 4.5 %copy-start.1 = (bf16[256,256]{1,0:T(8,128)(2,1)S(1)}, bf16[256,256]{1,0:T(8,128)(2,1)}, u32[]{:S(2)}) copy-start(bf16[256,256]{1,0:T(8,128)(2,1)} %param.11) | copy-start | bytes 393220
  327.0 3.9 %copy-start.26 = (f32[256,256]{1,0:T(8,128)S(1)}, f32[256,256]{1,0:T(8,128)}, u32[]{:S(2)}) copy-start(f32[256,256]{1,0:T(8,128)} %get-tuple-element.7) | copy-start | bytes 786436
Sparse Core Ops, SparseCore 0:
  12.8 80.4 all-reduce.8
  97.8 77.4 all-reduce.10
  220.9 105.9 all-reduce.12
Sparse Core Ops, SparseCore 1:
  16.5 13.1 all-gather.2
  193.2 10.0 all-gather.4
where the time goes:
time: 339 us
  waiting for transfers between devices  255 us (75%)
  matrix products  42.3 us (12%)
  between operations  15.5 us (5%)
  other arithmetic  11.2 us (3%)
  local copies, waits for them, and re-layouts  9.27 us (3%)
  starting transfers between devices  5.03 us (1%)
    psum x1, waiting for transfers between devices, on_device(): lax.psum((spatial_terms, temporal_terms, cond_terms), ('space', 'tm'))  91.7 us
    psum x1, waiting for transfers between devices, on_device(): cot_sum = lax.psum(jnp.sum(cot, axis=1, dtype=jnp.float32), 'space')  79.6 us
    psum x1, waiting for transfers between devices, from_root(): return lax.psum(block, axis)  75.7 us
    dot_general x9, matrix products, on_device(): lax.dot_general(piece, dpre, dims, preferred_element_type=jnp.float32)  11.9 us
    dot_general x18, matrix products, spatial_sum(): total = total + jnp.dot(piece, kernel, preferred_element_type=jnp.float32)  11.7 us
    ppermute x2, waiting for transfers between devices, shifted(): return lax.ppermute(value, axis, pairs)  7.84 us
  transfers between devices with their start and end apart: 7, of which 4 were waited for; matrix products, arithmetic and copies ran while one was open for 12% of the time, Pallas kernels for 0%

commit v1 on v0

--- a/solution.py
+++ b/solution.py
@@ -6,7 +6,7 @@
 
 def from_root(block, axis, source):
     block = jnp.where(lax.axis_index(axis) == source, block, jnp.zeros_like(block))
-    return lax.psum(block, axis)
+    return jnp.sum(lax.all_gather(block, axis), axis=0)
 
 
 def shifted(value, axis, by):

time: 339 us -> 320 us (0.944)
  waiting for transfers between devices: 255 us -> 222 us
  matrix products: 42.3 us -> 52.1 us
  other arithmetic: 11.2 us -> 14.9 us
    psum x1 -> x0, waiting for transfers between devices: 75.7 us -> none  [from_root(): return lax.psum(block, axis)]
    ppermute x2, waiting for transfers between devices: 7.84 us -> 60.3 us  [shifted(): return lax.ppermute(value, axis, pairs)]
    psum x1, waiting for transfers between devices: 79.6 us -> 61 us  [on_device(): cot_sum = lax.psum(jnp.sum(cot, axis=1, dtype=jnp.float32), 'space')]
    dot_general x18, matrix products: 11.7 us -> 28.7 us  [spatial_sum(): total = total + jnp.dot(piece, kernel, preferred_element_type=jnp.float32)]
    psum x1, waiting for transfers between devices: 91.7 us -> 101 us  [on_device(): lax.psum((spatial_terms, temporal_terms, cond_terms), ('space', 'tm'))]
    dot_general x9, matrix products: 11.9 us -> 4.35 us  [on_device(): lax.dot_general(piece, dpre, dims, preferred_element_type=jnp.float32)]
  transfers between devices with their start and end apart: 7 -> 7, of which waited for: 4 -> 4; matrix products, arithmetic and copies ran while one was open for 12% -> 18% of each run, Pallas kernels for 0% -> 0%
where the time goes in v1:
time: 320 us; the launch traced here: 319 us
  waiting for transfers between devices  222 us (69%)
  matrix products  52.1 us (16%)
  between operations  15.6 us (5%)
  other arithmetic  14.9 us (5%)
  local copies, waits for them, and re-layouts  9.43 us (3%)
  starting transfers between devices  5.1 us (2%)
    psum x1, waiting for transfers between devices, on_device(): lax.psum((spatial_terms, temporal_terms, cond_terms), ('space', 'tm'))  101 us
    psum x1, waiting for transfers between devices, on_device(): cot_sum = lax.psum(jnp.sum(cot, axis=1, dtype=jnp.float32), 'space')  61 us
    ppermute x2, waiting for transfers between devices, shifted(): return lax.ppermute(value, axis, pairs)  60.3 us
    dot_general x18, matrix products, spatial_sum(): total = total + jnp.dot(piece, kernel, preferred_element_type=jnp.float32)  28.7 us
    dot_general x3, matrix products, lag_backward(): jnp.dot(padded_cot[:, lag:lag + count], weights[lag].T, preferred_element...  6.59 us
  transfers between devices with their start and end apart: 7, of which 4 were waited for; matrix products, arithmetic and copies ran while one was open for 18% of the time, Pallas kernels for 0%

profile of v1, /device:TPU:0, one launch (start us, length us, event | category | flops | bytes accessed | tf_op | source)
XLA Modules:
  0.0 319.5 jit_solution(17368801483664651873)
XLA Ops:
  8.1 0.8 fusion.123
  8.9 2.3 broadcast_multiply_fusion.1
  11.3 1.4 convert_reduce_fusion
  12.7 1.3 collective-permute-start.1
  14.1 1.8 fusion.74
  15.9 28.7 %collective-permute-done.1 = bf16[2,2,2,256,256]{4,3,2,1,0:T(8,128)(2,1)S(1)} collective-permute-done((bf16[2,2,2,256,256]{4,3,2,1,0:T(8,128)(2,1)S(1)}, bf16[2,2,2,256,256]{4,3,2,1,0:T(8,128)(2,1)S(1)}, u32[]{:S(2)}, u32[]{:S(2)}) %collective-permute-start.1) | collective-permute-done | bytes 1048608 | tf_op jit(solution)/shard_map/ppermute | solution.py:15
  44.6 1.0 copy-done.22
  45.5 1.8 fusion.3
  47.4 1.8 pad_dynamic-slice_fusion.1
  49.2 0.5 fusion.38
  49.6 0.5 fusion.39
  50.1 0.5 fusion.40
  50.5 0.5 fusion.41
  51.0 0.5 fusion.42
  51.4 0.5 fusion.43
  51.9 0.4 fusion.58
  52.3 0.4 fusion.66
  52.8 2.2 multiply_convert_fusion.3
  54.9 0.4 copy-done.18
  55.4 0.3 copy-done.23
  55.7 3.0 multiply_convert_fusion.1
  58.7 2.0 slice_select_fusion
  60.8 61.0 %all-reduce.8.cloned.1.call-done = f32[2,2,256,256]{3,2,1,0:T(8,128)} async-done(((f32[2,2,256,256]{3,2,1,0:T(8,128)}), f32[2,2,256,256]{3,2,1,0:T(8,128)}) %all-reduce.8.cloned.1.call-update) | async-done | bytes 1048592 | tf_op jit(solution)/shard_map/psum | solution.py:101
  121.8 2.9 fusion.44
  124.7 3.6 %collective-permute-start = (bf16[2,2,2,256,256]{4,3,2,1,0:T(8,128)(2,1)S(1)}, bf16[2,2,2,256,256]{4,3,2,1,0:T(8,128)(2,1)S(1)}, u32[]{:S(2)}, u32[]{:S(2)}) collective-permute-start(bf16[2,2,2,256,256]{4,3,2,1,0:T(8,128)(2,1)S(1)} %copy-done.5), channel_id=1, source_target_pairs={{0,2},{2,4},{4,6},{6,8},{8,10},{10,12},{12,14},{1,3},{3,5},{5,7},{... | collective-permute-start | bytes 3145736 | tf_op jit(solution)/shard_map/ppermute | solution.py:15
  128.4 0.5 fusion.19
  128.9 0.5 fusion.12
  129.3 0.5 fusion.18
  129.8 0.5 fusion.17
  130.3 0.5 fusion.11
  130.8 0.5 fusion.16
  131.3 0.5 fusion.15
  131.8 0.7 copy-done.3
  132.5 0.5 convolution_bitcast_fusion.5
  133.0 0.5 fusion.10
  133.5 0.5 fusion.14
  134.0 0.5 copy-done.20
  134.5 2.1 fusion.76
  136.6 31.6 %collective-permute-done = bf16[2,2,2,256,256]{4,3,2,1,0:T(8,128)(2,1)S(1)} collective-permute-done((bf16[2,2,2,256,256]{4,3,2,1,0:T(8,128)(2,1)S(1)}, bf16[2,2,2,256,256]{4,3,2,1,0:T(8,128)(2,1)S(1)}, u32[]{:S(2)}, u32[]{:S(2)}) %collective-permute-start) | collective-permute-done | bytes 1048608 | tf_op jit(solution)/shard_map/ppermute | solution.py:15
  168.2 0.5 convolution_bitcast_fusion.4
  168.7 0.5 fusion.9
  169.1 1.0 pad_maximum_fusion.5
  170.1 1.7 fusion.7
  171.8 1.8 pad_dynamic-slice_fusion
  173.6 1.9 fusion.20
  175.5 1.8 fusion.22
  177.3 1.8 fusion.24
  179.1 1.8 fusion.26
  180.9 1.8 fusion.28
  182.8 1.9 fusion.30
  184.7 1.8 fusion.56
  186.5 1.8 fusion.64
  188.3 2.9 bitcast_reduce_fusion
  191.2 0.8 copy-done.11
  192.0 1.5 fusion.13
  193.5 1.2 copy-done.4
  194.7 8.4 %fusion.2 = bf16[2,2,2,256,256]{4,3,2,1,0:T(8,128)(2,1)} fusion(bf16[2,2,2,256,256]{4,3,2,1,0:T(8,128)(2,1)S(1)} %copy-done.4, f32[2,2,2,256,256]{4,3,2,1,0:T(8,128)} %fusion.20, f32[2,2,2,256,256]{4,3,2,1,0:T(8,128)} %fusion.22, f32[2,2,2,256,256]{4,3,2,1,0:T(8,128)} %fusion.24, f32[2,2,2,256,256]{4,3,2,1,0:T(8,128)} %fusion.56, ...), kind=kOutput, calls=%fused_computation.8 | convolution fusion | flops 275775488 | bytes 22151192 | tf_op jit(solution)/shard_map/dot_general | solution.py:32
  203.0 0.3 fusion.46
  203.4 0.9 copy-done.7
  204.3 2.6 multiply_convert_fusion.2
  206.8 101.0 %all-reduce.10.cloned.1.call-done = (f32[9,256,256]{2,1,0:T(8,128)}, f32[3,256,256]{2,1,0:T(8,128)}, f32[256,256]{1,0:T(8,128)}) async-done(((f32[9,256,256]{2,1,0:T(8,128)}, f32[3,256,256]{2,1,0:T(8,128)}, f32[256,256]{1,0:T(8,128)}), (f32[9,256,256]{2,1,0:T(8,128)}, f32[3,256,256]{2,1,0:T(8,128)}, f32[256,256]{1,0:T(8,128)})) %all-reduce.10.cloned.1.call-update) | async-done | bytes 3407888 | tf_op jit(solution)/shard_map/psum | solution.py:126
  307.8 3.0 multiply_convert_fusion
  310.9 0.8 multiply_convert_fusion.4
  311.7 0.7 multiply_convert_fusion.5
  (59 shorter events, 0.4 us)
Async XLA Ops:
  8.0 113.8 %copy-start = (bf16[256,256]{1,0:T(8,128)(2,1)S(1)}, bf16[256,256]{1,0:T(8,128)(2,1)}, u32[]{:S(2)}) copy-start(bf16[256,256]{1,0:T(8,128)(2,1)} %param.11) | copy-start | bytes 393220
  8.0 3.3 %copy-start.21 = (bf16[2,2,2,256,256]{4,3,2,1,0:T(8,128)(2,1)S(1)}, bf16[2,2,2,256,256]{4,3,2,1,0:T(8,128)(2,1)}, u32[]{:S(2)}) copy-start(bf16[2,2,2,256,256]{4,3,2,1,0:T(8,128)(2,1)} %param.7) | copy-start | bytes 3145732
  8.0 39.4 %all-gather.5.cloned.1.call-start = ((), (), s32[]{:S(2)}) async-start(), calls=%async_computation | async-start | bytes 3145728 | tf_op jit(solution)/shard_map/all_gather | solution.py:85
  11.3 2.8 copy-start.19
  11.3 110.6 %all-reduce.8.cloned.1.call-start = ((), (), s32[]{:S(2)}) async-start(), calls=%async_computation.2 | async-start | bytes 2097152 | tf_op jit(solution)/shard_map/psum | solution.py:101
  12.7 31.9 %copy-start.2 = (bf16[2,2,2,256,256]{4,3,2,1,0:T(8,128)(2,1)}, bf16[2,2,2,256,256]{4,3,2,1,0:T(8,128)(2,1)S(1)}, u32[]{:S(2)}) copy-start(bf16[2,2,2,256,256]{4,3,2,1,0:T(8,128)(2,1)S(1)} %get-tuple-element.9) | copy-start | bytes 3145732
  12.7 31.8 %collective-permute-start.1 = (bf16[2,2,2,256,256]{4,3,2,1,0:T(8,128)(2,1)S(1)}, bf16[2,2,2,256,256]{4,3,2,1,0:T(8,128)(2,1)S(1)}, u32[]{:S(2)}, u32[]{:S(2)}) collective-permute-start(bf16[2,2,2,256,256]{4,3,2,1,0:T(8,128)(2,1)S(1)} %get-tuple-element.9), channel_id=1, source_target_pairs={{2,0},{4,2},{6,4},{8,6},{10,8},{12,10},{14,12},{3,1},{5,3},{7,5},{... | collective-permute-start | bytes 3145736 | tf_op jit(solution)/shard_map/ppermute | solution.py:15
  14.0 157.8 %all-gather.7.cloned.1.call-start = ((), (), s32[]{:S(2)}) async-start(), calls=%async_computation.1 | async-start | bytes 3145728 | tf_op jit(solution)/shard_map/all_gather | solution.py:103
  44.6 1.0 copy-start.22
  47.4 1.8 copy-start.13
  52.7 2.2 copy-start.17
  52.8 2.6 copy-start.18
  52.8 2.9 copy-start.23
  58.7 69.7 %copy-start.1 = (bf16[2,2,2,256,256]{4,3,2,1,0:T(8,128)(2,1)S(1)}, bf16[2,2,2,256,256]{4,3,2,1,0:T(8,128)(2,1)}, u32[]{:S(2)}) copy-start(bf16[2,2,2,256,256]{4,3,2,1,0:T(8,128)(2,1)} %multiply_convert_fusion.1) | copy-start | bytes 3145732
  58.7 129.6 %all-gather.9.cloned.1.call-start = ((), (), s32[]{:S(2)}) async-start(), calls=%async_computation.3 | async-start | bytes 4718592 | tf_op jit(solution)/shard_map/all_gather | solution.py:9
  60.8 247.1 %all-reduce.10.cloned.1.call-start = ((), (), s32[]{:S(2)}) async-start(), calls=%async_computation.4 | async-start | bytes 6815744 | tf_op jit(solution)/shard_map/psum | solution.py:126
  121.8 2.9 copy-start.5
  124.7 43.4 %collective-permute-start = (bf16[2,2,2,256,256]{4,3,2,1,0:T(8,128)(2,1)S(1)}, bf16[2,2,2,256,256]{4,3,2,1,0:T(8,128)(2,1)S(1)}, u32[]{:S(2)}, u32[]{:S(2)}) collective-permute-start(bf16[2,2,2,256,256]{4,3,2,1,0:T(8,128)(2,1)S(1)} %copy-done.5), channel_id=1, source_target_pairs={{0,2},{2,4},{4,6},{6,8},{8,10},{10,12},{12,14},{1,3},{3,5},{5,7},{... | collective-permute-start | bytes 3145736 | tf_op jit(solution)/shard_map/ppermute | solution.py:15
  131.3 1.2 copy-start.3
  133.5 1.0 copy-start.20
  134.5 34.1 %copy-start.16 = (f32[9,256,256]{2,1,0:T(8,128)}, f32[9,256,256]{2,1,0:T(8,128)S(1)}, u32[]{:S(2)}) copy-start(f32[9,256,256]{2,1,0:T(8,128)S(1)} %fusion.14) | copy-start | bytes 7077892
  168.2 1.9 copy-start.6
  171.8 1.8 copy-start.14
  188.3 3.7 %copy-start.15 = (f32[2,2,256,256]{3,2,1,0:T(8,128)S(1)}, f32[2,2,256,256]{3,2,1,0:T(8,128)}, u32[]{:S(2)}) copy-start(f32[2,2,256,256]{3,2,1,0:T(8,128)} %all-reduce.8.cloned.1.call-done) | copy-start | bytes 3145732
  191.2 0.8 copy-start.11
  193.5 1.2 copy-start.4
  194.7 8.4 %copy-start.12 = (bf16[2,2,256,256]{3,2,1,0:T(8,128)(2,1)S(1)}, bf16[2,2,256,256]{3,2,1,0:T(8,128)(2,1)}, u32[]{:S(2)}) copy-start(bf16[2,2,256,256]{3,2,1,0:T(8,128)(2,1)} %copy-done.11) | copy-start | bytes 1572868
  194.7 8.7 %copy-start.8 = (bf16[2,2,2,256,256]{4,3,2,1,0:T(8,128)(2,1)S(1)}, bf16[2,2,2,256,256]{4,3,2,1,0:T(8,128)(2,1)}, u32[]{:S(2)}) copy-start(bf16[2,2,2,256,256]{4,3,2,1,0:T(8,128)(2,1)} %broadcast_multiply_fusion.1) | copy-start | bytes 3145732
  194.7 8.7 %copy-start.9 = (f32[2,2,2,256,256]{4,3,2,1,0:T(8,128)S(1)}, f32[2,2,2,256,256]{4,3,2,1,0:T(8,128)}, u32[]{:S(2)}) copy-start(f32[2,2,2,256,256]{4,3,2,1,0:T(8,128)} %fusion.76) | copy-start | bytes 6291460
  194.7 8.7 %copy-start.10 = (f32[2,2,2,256,256]{4,3,2,1,0:T(8,128)S(1)}, f32[2,2,2,256,256]{4,3,2,1,0:T(8,128)}, u32[]{:S(2)}) copy-start(f32[2,2,2,256,256]{4,3,2,1,0:T(8,128)} %fusion.7) | copy-start | bytes 6291460
  203.0 1.2 copy-start.7
  307.8 3.0 copy-start.24
  307.8 3.9 %copy-start.25 = (f32[256,256]{1,0:T(8,128)S(1)}, f32[256,256]{1,0:T(8,128)}, u32[]{:S(2)}) copy-start(f32[256,256]{1,0:T(8,128)} %get-tuple-element.7) | copy-start | bytes 786436
Sparse Core Ops, SparseCore 0:
  11.4 13.2 all-gather.4
  58.8 19.3 all-gather.6
  80.3 98.8 all-gather.8
Sparse Core Ops, SparseCore 1:
  15.8 106.0 all-reduce.7
  193.6 114.2 all-reduce.9
